TPU v7x, 512 devices: a whole 4x8x8 slice. The times are simulated.
512 devices in a mesh: seq: 128 (over x, z_hi, y, core), tp: 4 (over z_lo).
Axes of the slice: x: 4, y: 8, z: 8 (z_hi: 2, z_lo: 4; z = z_hi * 4 + z_lo), core: 2. Of those that a mesh axis runs over, the one named last changes fastest.
Arguments:
- queries: bfloat16 [16384, 4096], P('seq', 'tp'), may hold values from -6 to 6
- suffix_entries: bfloat16 [16384, 4096], P('seq', 'tp'), may hold values from -6 to 6
- prefix_cache: bfloat16 [2048, 4096], P(('seq', 'tp')), may hold values from -6 to 6
- block_prefix: int32 [512], replicated, may hold values from 0 to 1, as said below
- request_lengths: int32 [512], P('seq'), may hold values from 0 to 128, as said below
- request_prefix: int32 [512], P('seq'), may hold values from 0 to 1
Outputs:
- attended: bfloat16 [16384, 4096], P('seq', 'tp')
Inputs may be any that keep to these rules, and one draw needn't show every extreme that they name: `request_lengths`: the lengths of one index of seq's requests sum to at most 128; at some index they sum to exactly 128, and there one request alone takes all 128 slots. `block_prefix`: exactly half of the blocks belong to each prefix.
All inputs are finite; a program needn't handle non-finite values.
Results may differ from a plain program's by a relative error of at most 0.0049.
Values may be sent and summed in bfloat16 or wider, within the bound.
No kernel may reach another device: no remote copies, remote signals or barrier semaphores. Data moves between devices by JAX's collectives and lax.ppermute only.
A program may use at most 64 MiB of HBM per device.

v0:
```python
import math
import jax
import jax.numpy as jnp
import numpy as np
from jax import lax
from jax.sharding import Mesh
from jax.sharding import PartitionSpec as P

HEADS = 16
HEAD = 128
masked_score = -1e30
SEQ_PARTS = (("x", 4), ("zh", 2), ("y", 8), ("core", 2))
STAGES = (("x", "zh", "y"), ("core",))
TP_FIRST = "a2a"


def block_table(stages, per_block_rows, tensor_count):
    names = [n for n, _ in SEQ_PARTS]
    sizes = [s for _, s in SEQ_PARTS]
    coords = np.indices(sizes).reshape(len(sizes), -1).T
    seq_index = np.ravel_multi_index(coords.T, sizes)
    local = {}
    for c, s in zip(map(tuple, coords), seq_index):
        blocks = s * tensor_count + np.arange(tensor_count)
        local[c] = np.repeat(blocks, per_block_rows)
    gathered = set()
    for stage in stages:
        axes = [names.index(n) for n in stage]
        new = {}
        for c in local:
            parts = []
            for sub in np.ndindex(*[sizes[a] for a in axes]):
                other = list(c)
                for a, v in zip(axes, sub):
                    other[a] = v
                parts.append(local[tuple(other)])
            new[c] = np.concatenate(parts)
        local = new
        gathered.update(stage)
    tables = {tuple(v) for v in local.values()}
    assert len(tables) == 1
    return np.asarray(tables.pop(), np.int32)


def token_layout(lengths, prefixes, slots):
    cumulative = jnp.cumsum(lengths)
    slot_ids = jnp.arange(slots, dtype=jnp.int32)
    request_ids = jnp.sum((slot_ids[:, None] >= cumulative[None, :]).astype(jnp.int32), axis=1)
    live_slots = slot_ids < cumulative[-1]
    onehot = request_ids[:, None] == jnp.arange(lengths.shape[0], dtype=jnp.int32)[None, :]
    token_group = jnp.sum(jnp.where(onehot, prefixes[None, :], 0), axis=1)
    return (slot_ids, request_ids, live_slots, token_group)


def per_device(
    queries, suffix_entries, prefix_cache, block_prefix, request_lengths, request_prefix
):
    tensor_count = lax.axis_size("tp")
    local_heads = HEADS // tensor_count
    token_rows = queries.shape[0]
    block_rows = prefix_cache.shape[0]
    column_count = prefix_cache.shape[1] // tensor_count
    slot_ids, request_ids, live_slots, token_group = token_layout(
        request_lengths, request_prefix, token_rows
    )
    if TP_FIRST == "a2a":
        mine = lax.all_to_all(prefix_cache, "tp", split_axis=1, concat_axis=0, tiled=True)
    else:
        whole = lax.all_gather(prefix_cache, "tp", axis=0, tiled=True)
        start = lax.axis_index("tp") * column_count
        mine = lax.dynamic_slice_in_dim(whole, start, column_count, 1)
    for stage in STAGES:
        mine = lax.all_gather(mine, stage, axis=0, tiled=True)
    cached = mine.reshape(-1, local_heads, 2, HEAD)
    table = jnp.asarray(block_table(STAGES, block_rows, tensor_count))
    owners = jnp.take(block_prefix, table)
    query_rows = queries.reshape(token_rows, local_heads, 2, HEAD)
    own_entries = suffix_entries.reshape(token_rows, local_heads, 2, HEAD)
    scale = 1.0 / math.sqrt(HEAD)
    prefix_scores = (
        jnp.einsum(
            "thed,phd->thep", query_rows, cached[:, :, 0], preferred_element_type=jnp.float32
        )
        * scale
    )
    suffix_scores = (
        jnp.einsum(
            "thed,uhd->theu", query_rows, own_entries[:, :, 0], preferred_element_type=jnp.float32
        )
        * scale
    )
    prefix_allowed = ((token_group[:, None] == owners[None, :]) & live_slots[:, None])[
        :, None, None, :
    ]
    suffix_allowed = (
        (request_ids[:, None] == request_ids[None, :])
        & (slot_ids[None, :] <= slot_ids[:, None])
        & live_slots[:, None]
    )[:, None, None, :]
    prefix_scores = jnp.where(prefix_allowed, prefix_scores, masked_score)
    suffix_scores = jnp.where(suffix_allowed, suffix_scores, masked_score)
    row_max = jnp.maximum(jnp.max(prefix_scores, axis=-1), jnp.max(suffix_scores, axis=-1))
    prefix_weight = jnp.where(prefix_allowed, jnp.exp(prefix_scores - row_max[..., None]), 0.0)
    suffix_weight = jnp.where(suffix_allowed, jnp.exp(suffix_scores - row_max[..., None]), 0.0)
    total_weight = jnp.sum(prefix_weight, axis=-1) + jnp.sum(suffix_weight, axis=-1)
    weighted = jnp.einsum(
        "thep,phd->thed",
        prefix_weight.astype(jnp.bfloat16),
        cached[:, :, 1],
        preferred_element_type=jnp.float32,
    )
    weighted = weighted + jnp.einsum(
        "theu,uhd->thed",
        suffix_weight.astype(jnp.bfloat16),
        own_entries[:, :, 1],
        preferred_element_type=jnp.float32,
    )
    live_grid = live_slots[:, None, None]
    safe_total = jnp.where(live_grid, total_weight, 1.0)
    result = jnp.where(live_grid[..., None], weighted / safe_total[..., None], 0.0)
    return result.astype(jnp.bfloat16).reshape(token_rows, local_heads * 2 * HEAD)


def solution(mesh):
    sizes = tuple((s for _, s in SEQ_PARTS)) + (mesh.shape["tp"],)
    names = tuple((n for n, _ in SEQ_PARTS)) + ("tp",)
    fine = Mesh(mesh.devices.reshape(sizes), names)
    seq = names[:-1]
    in_specs = (P(seq, "tp"), P(seq, "tp"), P(seq + ("tp",), None), P(), P(seq), P(seq))
    out_specs = P(seq, "tp")
    return jax.shard_map(
        per_device, mesh=fine, in_specs=in_specs, out_specs=out_specs, check_vma=False
    )
```

profile of v0, /device:TPU:1, one launch (start us, length us, event | category | flops | bytes accessed | tf_op | source)
XLA Modules:
  0.0 202.8 jit_solution(8286302683828630251)
XLA Ops:
  6.5 12.4 %all_to_all.19 = bf16[4,4,1024]{2,0,1:T(4,128)(2,1)S(1)} all-to-all(bf16[4,4,1024]{2,0,1:T(4,128)(2,1)} %bitcast.71), channel_id=1, replica_groups=mesh['x'=4,'zh'=2,'y'=8,'core'=2,'tp'=4] {'tp'}, dimensions={1} | all-to-all | bytes 65536 | tf_op jit(solution)/shard_map/all_to_all | solution.py:67
  19.0 0.6 all_to_all.17
  19.6 0.0 all-gather.5.cloned.1.call-start
  19.7 137.8 %all-gather.3.cloned.1.call-done = bf16[1024,1024]{1,0:T(8,128)(2,1)} async-done(((bf16[16,1024]{1,0:T(8,128)(2,1)}), bf16[1024,1024]{1,0:T(8,128)(2,1)}) %all-gather.3.cloned.1.call-update) | async-done | bytes 2097168 | tf_op jit(solution)/shard_map/all_gather | solution.py:73
  157.5 0.8 reduce-window.4
  158.3 0.6 slice.16
  158.9 1.1 reshape.140
  160.0 1.1 copy.31
  161.2 0.7 broadcast_clamp_fusion
  161.9 13.2 %gather_fusion = s32[2048]{0:T(1024)S(1)} fusion(s32[512]{0:T(512)S(1)} %copy-done, s32[2048]{0:T(1024)S(1)} %broadcast_clamp_fusion), kind=kCustom, calls=%fused_computation | custom fusion | bytes 24576 | tf_op jit(solution)/shard_map/jit(_take)/gather | solution.py:76
  175.1 0.7 iota_compare_fusion.3
  175.7 0.1 convert_reduce_fusion
  175.8 0.1 select_reduce_fusion
  175.9 0.1 fusion.22
  176.0 0.3 fusion.27
  176.3 0.3 compare_and_fusion
  176.6 4.1 %all-gather.5.cloned.1.call-done = bf16[2048,1024]{1,0:T(8,128)(2,1)} async-done(((bf16[1024,1024]{1,0:T(8,128)(2,1)}), bf16[2048,1024]{1,0:T(8,128)(2,1)}) %all-gather.5.cloned.1.call-update) | async-done | bytes 4194320 | tf_op jit(solution)/shard_map/all_gather | solution.py:73
  180.7 6.5 %copy.28 = bf16[2048,1024]{0,1:T(8,128)(2,1)} copy(bf16[2048,1024]{1,0:T(8,128)(2,1)} %all-gather.5.cloned.1.call-done) | data formatting | bytes 8388608 | tf_op jit(solution)/shard_map/all_gather | solution.py:73
  187.3 3.3 %fusion = (f32[128,4,2]{0,2,1:T(2,128)S(1)}, f32[4,2048,128,2]{2,1,3,0:T(8,128)S(1)}) fusion(pred[128,2048]{0,1:T(8,128)(4,1)S(1)} %compare_and_fusion, bf16[128,4,2,128]{3,2,1,0:T(2,128)(2,1)S(1)} %reshape.140, bf16[2048,4,2,128]{0,3,2,1:T(8,128)(2,1)} %bitcast.65), kind=kOutput, calls=%fused_computation.3 | convolution fusion | flops 543161344 | bytes 11014144 | tf_op jit(solution)/shard_map/thed,phd->thep/dot_general | solution.py:81
  190.6 2.1 %fusion.3 = f32[4,128,2,128]{1,3,2,0:T(8,128)S(1)} fusion(f32[4,2048,128,2]{2,1,3,0:T(8,128)S(1)} %get-tuple-element.6, f32[128,4,2]{0,2,1:T(2,128)S(1)} %max.7, pred[128,2048]{0,1:T(8,128)(4,1)S(1)} %compare_and_fusion, bf16[2048,4,2,128]{0,3,2,1:T(8,128)(2,1)S(1)} %bitcast.66), kind=kOutput, calls=%fused_computation.6 | convolution fusion | flops 547356672 | bytes 11276288 | tf_op jit(solution)/shard_map/thep,phd->thed/dot_general | solution.py:106
  192.7 2.0 %fusion.1 = f32[128,4,2]{0,2,1:T(2,128)S(1)} fusion(f32[4,2048,128,2]{2,1,3,0:T(8,128)S(1)} %get-tuple-element.6, f32[128,4,2]{0,2,1:T(2,128)S(1)} %max.7, pred[128,2048]{0,1:T(8,128)(4,1)S(1)} %compare_and_fusion), kind=kLoop, calls=%fused_computation.4 | loop fusion | flops 10484736 | bytes 8658944 | tf_op jit(solution)/shard_map/reduce_sum | solution.py:105
  194.7 0.1 fusion.13
  194.9 0.3 fusion.12
  195.1 0.9 copy.38
  (11 shorter events, 0.1 us)
Async XLA Ops:
  6.5 155.3 %copy-start = (s32[512]{0:T(512)S(1)}, s32[512]{0:T(512)}, u32[]{:S(2)}) copy-start(s32[512]{0:T(512)} %param.10) | copy-start | bytes 6148
  6.5 169.3 %copy-start.2 = (s32[4]{0:T(128)S(1)}, s32[4]{0:T(128)}, u32[]{:S(2)}) copy-start(s32[4]{0:T(128)} %param.12) | copy-start | bytes 52
  6.5 150.9 %all-gather.3.cloned.1.call-start = ((), (), s32[]{:S(2)}) async-start(), calls=%async_computation.1 | async-start | bytes 2129920 | tf_op jit(solution)/shard_map/all_gather | solution.py:73
  19.6 161.1 %all-gather.5.cloned.1.call-start = ((), (), s32[]{:S(2)}) async-start(), calls=%async_computation.2 | async-start | bytes 6291456 | tf_op jit(solution)/shard_map/all_gather | solution.py:73
  187.3 3.4 %copy-start.1 = (bf16[2048,1024]{0,1:T(8,128)(2,1)S(1)}, bf16[2048,1024]{0,1:T(8,128)(2,1)}, u32[]{:S(2)}) copy-start(bf16[2048,1024]{0,1:T(8,128)(2,1)} %copy.28) | copy-start | bytes 12582916
Sparse Core Ops, SparseCore 0:
  19.7 137.6 all-gather.2
  159.6 21.1 all-gather.4
where the time goes:
time: 203 us
  waiting for transfers between devices  142 us (70%)
  local copies, waits for them, and re-layouts  24 us (12%)
  between operations  13.5 us (7%)
  blocking collectives  12.4 us (6%)
  matrix products  5.95 us (3%)
  other arithmetic  4.94 us (2%)
    all_gather x2, waiting for transfers between devices, per_device(): mine = lax.all_gather(mine, stage, axis=0, tiled=True)  142 us
    gather x1, local copies, waits for them, and re-layouts, per_device(): owners = jnp.take(block_prefix, table)  13.2 us
    all_to_all x1, blocking collectives, per_device(): lax.all_to_all(prefix_cache, 'tp', split_axis=1, concat_axis=0, tiled=True)  12.4 us
    all_gather x1, local copies, waits for them, and re-layouts, per_device(): mine = lax.all_gather(mine, stage, axis=0, tiled=True)  6.52 us
  transfers between devices with their start and end apart: 2, of which 2 were waited for; matrix products, arithmetic and copies ran while one was open for 9% of the time, Pallas kernels for 0%

commit v1 on v0

--- a/solution.py
+++ b/solution.py
@@ -70,7 +70,9 @@
         start = lax.axis_index("tp") * column_count
         mine = lax.dynamic_slice_in_dim(whole, start, column_count, 1)
     for stage in STAGES:
-        mine = lax.all_gather(mine, stage, axis=0, tiled=True)
+        mine = jnp.concatenate(
+            lax.all_to_all(jnp.stack([mine] * lax.axis_size(stage)), stage, 0, 0), axis=0
+        )
     cached = mine.reshape(-1, local_heads, 2, HEAD)
     table = jnp.asarray(block_table(STAGES, block_rows, tensor_count))
     owners = jnp.take(block_prefix, table)

time: 203 us -> 130 us (0.64)
  waiting for transfers between devices: 142 us -> 31.5 us
  local copies, waits for them, and re-layouts: 24 us -> 45 us
  starting transfers between devices: 0.04 us -> 16 us
  between operations: 13.5 us -> 0.12 us
  blocking collectives: 12.4 us -> 24.9 us
    all_gather x2 -> x0, waiting for transfers between devices: 142 us -> none  [per_device(): mine = lax.all_gather(mine, stage, axis=0, tiled=True)]
    all_to_all x0 -> x1, waiting for transfers between devices: none -> 31.5 us  [per_device(): lax.all_to_all(jnp.stack([mine] * lax.axis_size(stage)), stage, 0, 0)]
    all_to_all x0 -> x1, starting transfers between devices: none -> 16 us  [per_device(): lax.all_to_all(jnp.stack([mine] * lax.axis_size(stage)), stage, 0, 0)]
    all_to_all x0 -> x1, blocking collectives: none -> 12.4 us  [per_device(): lax.all_to_all(jnp.stack([mine] * lax.axis_size(stage)), stage, 0, 0)]
    slice x0 -> x1, local copies, waits for them, and re-layouts: none -> 9.77 us  [per_device(): cached[:, :, 1]]
    another operation x0 -> x3, local copies, waits for them, and re-layouts: none -> 9.34 us  [the longest x1 7.71 us: per_device(): cached = mine.reshape(-1, local_heads, 2, HEAD)]
    unnamed x7 -> x6, local copies, waits for them, and re-layouts: 1.13 us -> 10.1 us
    all_gather x1 -> x0, local copies, waits for them, and re-layouts: 6.52 us -> none  [per_device(): mine = lax.all_gather(mine, stage, axis=0, tiled=True)]
  transfers between devices with their start and end apart: 2 -> 1, of which waited for: 2 -> 1; matrix products, arithmetic and copies ran while one was open for 9% -> 15% of each run, Pallas kernels for 0% -> 0%
where the time goes in v1:
time: 130 us; the launch traced here: 129 us
  local copies, waits for them, and re-layouts  45 us (35%)
  waiting for transfers between devices  31.5 us (24%)
  blocking collectives  24.9 us (19%)
  starting transfers between devices  16 us (12%)
  matrix products  6.37 us (5%)
  other arithmetic  5.3 us (4%)
    all_to_all x1, waiting for transfers between devices, per_device(): lax.all_to_all(jnp.stack([mine] * lax.axis_size(stage)), stage, 0, 0)  31.5 us
    all_to_all x1, starting transfers between devices, per_device(): lax.all_to_all(jnp.stack([mine] * lax.axis_size(stage)), stage, 0, 0)  16 us
    gather x1, local copies, waits for them, and re-layouts, per_device(): owners = jnp.take(block_prefix, table)  13.2 us
    all_to_all x1, blocking collectives, per_device(): lax.all_to_all(jnp.stack([mine] * lax.axis_size(stage)), stage, 0, 0)  12.4 us
    all_to_all x1, blocking collectives, per_device(): lax.all_to_all(prefix_cache, 'tp', split_axis=1, concat_axis=0, tiled=True)  12.4 us
    unnamed x6, local copies, waits for them, and re-layouts  10.1 us
    slice x1, local copies, waits for them, and re-layouts, per_device(): cached[:, :, 1]  9.77 us
    another operation x1, local copies, waits for them, and re-layouts, per_device(): cached = mine.reshape(-1, local_heads, 2, HEAD)  7.71 us
  transfers between devices with their start and end apart: 1, of which 1 were waited for; matrix products, arithmetic and copies ran while one was open for 15% of the time, Pallas kernels for 0%

profile of v1, /device:TPU:1, one launch (start us, length us, event | category | flops | bytes accessed | tf_op | source)
XLA Modules:
  0.0 129.1 jit_solution(12570581258516083177)
XLA Ops:
  0.0 12.4 %all_to_all.26 = bf16[4,4,1024]{2,0,1:T(4,128)(2,1)S(1)} all-to-all(bf16[4,4,1024]{2,0,1:T(4,128)(2,1)} %bitcast.75), channel_id=1, replica_groups=mesh['x'=4,'zh'=2,'y'=8,'core'=2,'tp'=4] {'tp'}, dimensions={1} | all-to-all | bytes 65536 | tf_op jit(solution)/shard_map/all_to_all | solution.py:67
  12.5 1.6 %stack.7 = bf16[64,16,1024]{2,1,0:T(8,128)(2,1)} broadcast(bf16[16,1024]{1,0:T(8,128)(2,1)S(1)} %stack.6), dimensions={1,2} | broadcast | bytes 2129920 | tf_op jit(solution)/shard_map/stack | solution.py:74
  14.1 16.0 %all-to-all-start.1 = ((bf16[64,16,1024]{2,1,0:T(8,128)(2,1)}), bf16[64,16,1024]{2,1,0:T(8,128)(2,1)S(1)}, u32[]{:S(2)}, u32[]{:S(2)}) async-start(bf16[64,16,1024]{2,1,0:T(8,128)(2,1)} %stack.7), calls=%async_computation.1 | async-start | bytes 4194304 | tf_op jit(solution)/shard_map/all_to_all | solution.py:74
  30.1 0.8 reduce-window.4
  30.9 0.6 slice.16
  31.5 1.1 reshape.139
  32.6 1.1 copy.30
  33.8 0.7 broadcast_clamp_fusion
  34.5 13.2 %gather_fusion = s32[2048]{0:T(1024)S(1)} fusion(s32[512]{0:T(512)S(1)} %copy-done, s32[2048]{0:T(1024)S(1)} %broadcast_clamp_fusion), kind=kCustom, calls=%fused_computation | custom fusion | bytes 24576 | tf_op jit(solution)/shard_map/jit(_take)/gather | solution.py:78
  47.7 0.7 iota_compare_fusion.3
  48.6 0.3 fusion.34
  48.9 0.3 compare_and_fusion
  49.2 31.5 %all-to-all-done.1 = bf16[64,16,1024]{2,1,0:T(8,128)(2,1)S(1)} async-done(((bf16[64,16,1024]{2,1,0:T(8,128)(2,1)}), bf16[64,16,1024]{2,1,0:T(8,128)(2,1)S(1)}, u32[]{:S(2)}, u32[]{:S(2)}) %all-to-all-start.1) | async-done | bytes 2097184 | tf_op jit(solution)/shard_map/all_to_all | solution.py:74
  80.7 0.4 pad_maximum_fusion
  81.1 12.4 %all_to_all.27 = bf16[2,1024,1024]{2,1,0:T(8,128)(2,1)} all-to-all(bf16[2,1024,1024]{2,1,0:T(8,128)(2,1)S(1)} %pad_maximum_fusion), channel_id=1, replica_groups=mesh['x'=4,'zh'=2,'y'=8,'core'=2,'tp'=4] {'core'}, dimensions={0} | all-to-all | bytes 8388608 | tf_op jit(solution)/shard_map/all_to_all | solution.py:74
  93.5 7.7 %reshape_reshape.3 = bf16[2048,4,2,128]{3,2,1,0:T(2,128)(2,1)} reshape(bf16[2,1024,1024]{2,1,0:T(8,128)(2,1)} %all_to_all.27) | data formatting | bytes 8388608 | tf_op jit(solution)/shard_map/reshape;reshape | solution.py:76
  101.2 9.8 %fusion.33 = (bf16[2048,4,1,128]{3,2,1,0:T(2,128)(2,1)}, bf16[2048,4,1,128]{3,2,1,0:T(2,128)(2,1)}) fusion(bf16[2048,4,2,128]{3,2,1,0:T(2,128)(2,1)} %reshape_reshape.3), kind=kLoop, calls=%fused_computation.46 | loop fusion | bytes 8388608 | tf_op jit(solution)/shard_map/slice | solution.py:111
  111.0 9.0 %copy.43 = bf16[2048,4,1,128]{0,3,1,2:T(8,128)(2,1)S(1)} copy(bf16[2048,4,1,128]{3,2,1,0:T(2,128)(2,1)} %get-tuple-element.5) | data formatting | bytes 4194304
  120.0 3.7 %fusion = (f32[128,4,2]{0,2,1:T(2,128)S(1)}, f32[4,2048,128,2]{2,1,3,0:T(8,128)S(1)}) fusion(pred[128,2048]{0,1:T(8,128)(4,1)S(1)} %compare_and_fusion, bf16[128,4,2,128]{3,2,1,0:T(2,128)(2,1)S(1)} %reshape.139, bf16[2048,4,1,128]{3,2,1,0:T(2,128)(2,1)} %get-tuple-element.6), kind=kOutput, calls=%fused_computation.3 | convolution fusion | flops 543161344 | bytes 11014144 | tf_op jit(solution)/shard_map/thed,phd->thep/dot_general | solution.py:83
  123.7 2.0 %fusion.1 = f32[128,4,2]{0,2,1:T(2,128)S(1)} fusion(f32[4,2048,128,2]{2,1,3,0:T(8,128)S(1)} %get-tuple-element.8, f32[128,4,2]{0,2,1:T(2,128)S(1)} %max.7, pred[128,2048]{0,1:T(8,128)(4,1)S(1)} %compare_and_fusion), kind=kLoop, calls=%fused_computation.4 | loop fusion | flops 10484736 | bytes 8658944 | tf_op jit(solution)/shard_map/reduce_sum | solution.py:107
  125.7 2.1 %fusion.13 = f32[128,4,2,128]{0,3,2,1:T(8,128)S(1)} fusion(f32[4,2048,128,2]{2,1,3,0:T(8,128)S(1)} %get-tuple-element.8, f32[128,4,2]{0,2,1:T(2,128)S(1)} %max.7, pred[128,2048]{0,1:T(8,128)(4,1)S(1)} %compare_and_fusion, bf16[2048,4,1,128]{0,3,1,2:T(8,128)(2,1)S(1)} %copy.43), kind=kOutput, calls=%fused_computation.19 | convolution fusion | flops 547356672 | bytes 11276288 | tf_op jit(solution)/shard_map/thep,phd->thed/dot_general | solution.py:108
  127.9 0.1 fusion.19
  128.0 0.3 fusion.18
  128.3 0.9 copy.36
  (10 shorter events, 0.3 us)
Async XLA Ops:
  0.0 34.5 %copy-start = (s32[512]{0:T(512)S(1)}, s32[512]{0:T(512)}, u32[]{:S(2)}) copy-start(s32[512]{0:T(512)} %param.10) | copy-start | bytes 6148
  0.0 48.4 %copy-start.1 = (s32[4]{0:T(128)S(1)}, s32[4]{0:T(128)}, u32[]{:S(2)}) copy-start(s32[4]{0:T(128)} %param.12) | copy-start | bytes 52
  14.1 66.7 %all-to-all-start.1 = ((bf16[64,16,1024]{2,1,0:T(8,128)(2,1)}), bf16[64,16,1024]{2,1,0:T(8,128)(2,1)S(1)}, u32[]{:S(2)}, u32[]{:S(2)}) async-start(bf16[64,16,1024]{2,1,0:T(8,128)(2,1)} %stack.7), calls=%async_computation.1 | async-start | bytes 4194304 | tf_op jit(solution)/shard_map/all_to_all | solution.py:74

commit v2 on v0

--- a/solution.py
+++ b/solution.py
@@ -64,7 +64,12 @@
         request_lengths, request_prefix, token_rows
     )
     if TP_FIRST == "a2a":
-        mine = lax.all_to_all(prefix_cache, "tp", split_axis=1, concat_axis=0, tiled=True)
+        mine = jnp.concatenate(
+            lax.all_to_all(
+                jnp.stack(jnp.split(prefix_cache, lax.axis_size("tp"), axis=1)), "tp", 0, 0
+            ),
+            axis=0,
+        )
     else:
         whole = lax.all_gather(prefix_cache, "tp", axis=0, tiled=True)
         start = lax.axis_index("tp") * column_count

time: 203 us -> 204 us (level)
  no operation moved by 1% of the time
where the time goes in v2:
time: 204 us; the launch traced here: 203 us
  waiting for transfers between devices  142 us (70%)
  local copies, waits for them, and re-layouts  24.8 us (12%)
  between operations  13.5 us (7%)
  blocking collectives  12.1 us (6%)
  matrix products  5.95 us (3%)
  other arithmetic  4.98 us (2%)
    all_gather x2, waiting for transfers between devices, per_device(): mine = lax.all_gather(mine, stage, axis=0, tiled=True)  142 us
    gather x1, local copies, waits for them, and re-layouts, per_device(): owners = jnp.take(block_prefix, table)  13.2 us
    all_to_all x1, blocking collectives, per_device(): lax.all_to_all(jnp.stack(jnp.split(prefix_cache, lax.axis_size('tp'), axi...  12.1 us
    all_gather x1, local copies, waits for them, and re-layouts, per_device(): mine = lax.all_gather(mine, stage, axis=0, tiled=True)  6.52 us
  transfers between devices with their start and end apart: 2, of which 2 were waited for; matrix products, arithmetic and copies ran while one was open for 9% of the time, Pallas kernels for 0%

profile of v2, /device:TPU:1, one launch (start us, length us, event | category | flops | bytes accessed | tf_op | source)
XLA Modules:
  0.0 203.3 jit_solution(12531746443858411171)
XLA Ops:
  6.5 0.8 slice_bitcast_fusion.13
  7.4 12.1 %all_to_all.5 = bf16[4,4,1024]{2,1,0:T(4,128)(2,1)S(1)} all-to-all(bf16[4,4,1024]{2,1,0:T(4,128)(2,1)S(1)} %pad_maximum_fusion), channel_id=1, replica_groups=mesh['x'=4,'zh'=2,'y'=8,'core'=2,'tp'=4] {'tp'}, dimensions={0} | all-to-all | bytes 65536 | tf_op jit(solution)/shard_map/all_to_all | solution.py:68
  19.5 0.6 reshape.139
  20.2 137.8 %all-gather.3.cloned.1.call-done = bf16[1024,1024]{1,0:T(8,128)(2,1)} async-done(((bf16[16,1024]{1,0:T(8,128)(2,1)}), bf16[1024,1024]{1,0:T(8,128)(2,1)}) %all-gather.3.cloned.1.call-update) | async-done | bytes 2097168 | tf_op jit(solution)/shard_map/all_gather | solution.py:78
  158.0 0.8 reduce-window.4
  158.8 0.6 slice.16
  159.4 1.1 reshape.141
  160.5 1.1 copy.41
  161.6 0.7 broadcast_clamp_fusion
  162.4 13.2 %gather_fusion = s32[2048]{0:T(1024)S(1)} fusion(s32[512]{0:T(512)S(1)} %copy-done, s32[2048]{0:T(1024)S(1)} %broadcast_clamp_fusion), kind=kCustom, calls=%fused_computation | custom fusion | bytes 24576 | tf_op jit(solution)/shard_map/jit(_take)/gather | solution.py:81
  175.5 0.7 iota_compare_fusion.3
  176.2 0.1 convert_reduce_fusion
  176.3 0.1 select_reduce_fusion
  176.4 0.1 fusion.25
  176.5 0.3 fusion.30
  176.8 0.3 compare_and_fusion
  177.1 4.1 %all-gather.5.cloned.1.call-done = bf16[2048,1024]{1,0:T(8,128)(2,1)} async-done(((bf16[1024,1024]{1,0:T(8,128)(2,1)}), bf16[2048,1024]{1,0:T(8,128)(2,1)}) %all-gather.5.cloned.1.call-update) | async-done | bytes 4194320 | tf_op jit(solution)/shard_map/all_gather | solution.py:78
  181.2 6.5 %copy.37 = bf16[2048,1024]{0,1:T(8,128)(2,1)} copy(bf16[2048,1024]{1,0:T(8,128)(2,1)} %all-gather.5.cloned.1.call-done) | data formatting | bytes 8388608 | tf_op jit(solution)/shard_map/all_gather | solution.py:78
  187.8 3.3 %fusion = (f32[128,4,2]{0,2,1:T(2,128)S(1)}, f32[4,2048,128,2]{2,1,3,0:T(8,128)S(1)}) fusion(pred[128,2048]{0,1:T(8,128)(4,1)S(1)} %compare_and_fusion, bf16[128,4,2,128]{3,2,1,0:T(2,128)(2,1)S(1)} %reshape.141, bf16[2048,4,2,128]{0,3,2,1:T(8,128)(2,1)} %bitcast.79), kind=kOutput, calls=%fused_computation.3 | convolution fusion | flops 543161344 | bytes 11014144 | tf_op jit(solution)/shard_map/thed,phd->thep/dot_general | solution.py:86
  191.1 2.1 %fusion.12 = f32[128,4,2,128]{0,3,2,1:T(8,128)S(1)} fusion(f32[4,2048,128,2]{2,1,3,0:T(8,128)S(1)} %get-tuple-element.10, f32[128,4,2]{0,2,1:T(2,128)S(1)} %max.7, pred[128,2048]{0,1:T(8,128)(4,1)S(1)} %compare_and_fusion, bf16[2048,4,2,128]{0,3,2,1:T(8,128)(2,1)S(1)} %bitcast.80), kind=kOutput, calls=%fused_computation.18 | convolution fusion | flops 547356672 | bytes 11276288 | tf_op jit(solution)/shard_map/thep,phd->thed/dot_general | solution.py:111
  193.2 2.0 %fusion.1 = f32[128,4,2]{0,2,1:T(2,128)S(1)} fusion(f32[4,2048,128,2]{2,1,3,0:T(8,128)S(1)} %get-tuple-element.10, f32[128,4,2]{0,2,1:T(2,128)S(1)} %max.7, pred[128,2048]{0,1:T(8,128)(4,1)S(1)} %compare_and_fusion), kind=kLoop, calls=%fused_computation.4 | loop fusion | flops 10484736 | bytes 8658944 | tf_op jit(solution)/shard_map/reduce_sum | solution.py:110
  195.2 0.1 fusion.16
  195.4 0.3 fusion.15
  195.6 0.9 copy.47
  (13 shorter events, 0.1 us)
Async XLA Ops:
  6.5 155.8 %copy-start = (s32[512]{0:T(512)S(1)}, s32[512]{0:T(512)}, u32[]{:S(2)}) copy-start(s32[512]{0:T(512)} %param.10) | copy-start | bytes 6148
  6.5 169.8 %copy-start.2 = (s32[4]{0:T(128)S(1)}, s32[4]{0:T(128)}, u32[]{:S(2)}) copy-start(s32[4]{0:T(128)} %param.12) | copy-start | bytes 52
  6.5 151.4 %all-gather.3.cloned.1.call-start = ((), (), s32[]{:S(2)}) async-start(), calls=%async_computation.1 | async-start | bytes 2129920 | tf_op jit(solution)/shard_map/all_gather | solution.py:78
  20.1 161.1 %all-gather.5.cloned.1.call-start = ((), (), s32[]{:S(2)}) async-start(), calls=%async_computation.2 | async-start | bytes 6291456 | tf_op jit(solution)/shard_map/all_gather | solution.py:78
  187.8 3.4 %copy-start.1 = (bf16[2048,1024]{0,1:T(8,128)(2,1)S(1)}, bf16[2048,1024]{0,1:T(8,128)(2,1)}, u32[]{:S(2)}) copy-start(bf16[2048,1024]{0,1:T(8,128)(2,1)} %copy.37) | copy-start | bytes 12582916
Sparse Core Ops, SparseCore 0:
  20.2 137.6 all-gather.2
  160.1 21.1 all-gather.4
